TPU v7x, 512 devices: a whole 4x8x8 slice. The times are simulated.
512 devices in a mesh: section: 8 (over y), dp: 64 (over x, z, core).
Axes of the slice: x: 4, y: 8, z: 8, core: 2. Of those that a mesh axis runs over, the one named last changes fastest.
Arguments:
- queries: bfloat16 [65536, 3584], P(('section', 'dp')), may hold values from -1 to 1
- passages: bfloat16 [128, 64, 3584], P('dp'), may hold values from -1 to 1
- candidates: int32 [512, 3], P('section'), may hold values from 0 to 63, as said below
- counts: int32 [512], P('section'), may hold values from 1 to 3, 1024 in all
- teacher: float32 [65536, 384], P(('section', 'dp')), may hold values from -20 to 450
- section_weights: bfloat16 [8, 3584, 3584], P('section', 'dp'), may hold values from -0.09375 to 0.09375
- section_inputs: bfloat16 [8, 64, 3584], P('section', None, 'dp'), may hold values from -1.5 to 1.5
- pre_acts: bfloat16 [8, 64, 3584], P('section', None, 'dp'), may hold values from -8 to 8
Outputs:
- query_grads: bfloat16 [65536, 3584], P(('section', 'dp'))
- passage_grads: bfloat16 [128, 64, 3584], P('dp')
- grad_inputs: float32 [8, 64, 3584], P('section', None, 'dp')
- weight_grads: bfloat16 [8, 3584, 3584], P('section', 'dp')
Inputs may be any that keep to these rules, and one draw needn't show every extreme that they name: `candidates`: each row names 3 different passage blocks. A query block uses the first counts[b] entries of its row of candidates.
All inputs are finite; a program needn't handle non-finite values.
Results may differ from a plain program's by a relative error of at most 0.0085.
Values may be sent and summed in bfloat16 or wider, within the bound.
No kernel may reach another device: no remote copies, remote signals or barrier semaphores. Data moves between devices by JAX's collectives and lax.ppermute only.
A program may use at most 64 MiB of HBM per device.

v0:
```python
import jax
import jax.numpy as jnp
from jax import lax
from jax.sharding import PartitionSpec as P

INVERSE_TEMP = 20.0


def passed_along(value, axis, steps):
    count = lax.axis_size(axis)
    initial, last = (max(0, -steps), min(count, count - steps))
    return lax.ppermute(value, axis, [(source, source + steps) for source in range(initial, last)])


def gathered_pieces(value, axis):
    count = lax.axis_size(axis)
    copies = jnp.broadcast_to(value[None], (count,) + value.shape)
    return lax.all_to_all(copies, axis, 0, 0, tiled=True)


def gathered_columns(value, axis):
    count = lax.axis_size(axis)
    copies = jnp.broadcast_to(value[None], (count,) + value.shape)
    pieces = lax.all_to_all(copies, axis, 0, 0, tiled=True)
    return jnp.transpose(pieces, (1, 0, 2)).reshape(value.shape[0], count * value.shape[1])


def soft_weights(logits, valid):
    masked = jnp.where(valid, logits, -1e30)
    highest = jnp.max(masked, axis=-1, keepdims=True)
    expons = jnp.where(valid, jnp.exp(masked - highest), 0.0)
    return expons / jnp.sum(expons, axis=-1, keepdims=True)


def body(queries, passages, candidates, counts, teacher, section_weights, section_inputs, pre_acts):
    dp_count = lax.axis_size("dp")
    dp_index = lax.axis_index("dp")
    stripe, block_total, width = passages.shape
    row_block_count = stripe * dp_count
    blocks_here = candidates.shape[0] // dp_count
    slot_count = candidates.shape[1]
    requests = blocks_here * slot_count
    all_slots = candidates.reshape(-1)
    chooser = (all_slots[:, None] == jnp.arange(block_total, dtype=jnp.int32)[None, :]).astype(
        passages.dtype
    )
    outgoing = jnp.einsum(
        "rpj,sp->rsj", passages, chooser, preferred_element_type=jnp.float32
    ).astype(passages.dtype)
    pulled_rows = lax.all_to_all(outgoing, "dp", split_axis=1, concat_axis=0, tiled=True)
    pulled_rows = pulled_rows.reshape(row_block_count, blocks_here, slot_count, width)
    own_counts = lax.dynamic_slice_in_dim(counts, dp_index * blocks_here, blocks_here)
    slot_valid = jnp.arange(slot_count, dtype=jnp.int32)[None, :] < own_counts[:, None]
    column_valid = jnp.repeat(slot_valid, row_block_count, axis=1)[:, None, :]
    query_row_items = queries.reshape(blocks_here, row_block_count, width)
    logits = (
        jnp.einsum(
            "ixp,wifp->ixfw", query_row_items, pulled_rows, preferred_element_type=jnp.float32
        )
        * INVERSE_TEMP
    )
    logits = logits.reshape(blocks_here, row_block_count, slot_count * row_block_count)
    target_logits = soft_weights(
        teacher.reshape(blocks_here, row_block_count, slot_count * row_block_count), column_valid
    )
    weight_matrices = (soft_weights(logits, column_valid) - target_logits).astype(jnp.bfloat16)
    weight_matrices = weight_matrices.reshape(
        blocks_here, row_block_count, slot_count, row_block_count
    )
    query_sums = (
        jnp.einsum(
            "geal,lgay->gey", weight_matrices, pulled_rows, preferred_element_type=jnp.float32
        )
        * INVERSE_TEMP
    )
    passage_sums = (
        jnp.einsum(
            "fnyw,fnj->wfyj", weight_matrices, query_row_items, preferred_element_type=jnp.float32
        )
        * INVERSE_TEMP
    )
    block_terms = passage_sums.reshape(row_block_count, requests, width).astype(jnp.bfloat16)
    micro_count = section_inputs.shape[1] // dp_count
    col_width = width // dp_count
    micro_cols = jnp.transpose(
        query_sums[0, :micro_count].reshape(micro_count, dp_count, col_width), (1, 0, 2)
    )
    section_count = lax.axis_size("section")
    chunk = width // section_count
    term_pieces = passage_sums.reshape(dp_count, stripe, requests, section_count, chunk)
    term_pieces = jnp.transpose(term_pieces, (3, 0, 1, 2, 4)).astype(jnp.bfloat16)
    term_pieces = term_pieces.reshape(section_count * dp_count, stripe, requests, chunk)
    own_slots = lax.dynamic_slice_in_dim(all_slots, dp_index * requests, requests)
    slot_tags = jnp.broadcast_to(
        own_slots.astype(jnp.bfloat16)[None, None, :, None],
        (section_count * dp_count, stripe, requests, 1),
    )
    term_pieces = jnp.concatenate([term_pieces, slot_tags], axis=3)
    incoming_terms = lax.all_to_all(
        term_pieces, ("section", "dp"), split_axis=0, concat_axis=0, tiled=True
    )
    last_section = section_count - 1
    packed = jnp.concatenate(
        [section_weights[0].reshape(col_width, dp_count, col_width), pre_acts[0][None]]
    )
    moved = tuple(
        (
            lax.ppermute(packed, "section", [(source, last_section)])
            for source in range(last_section)
        )
    )
    incoming_terms, carry_start, moved = lax.optimization_barrier(
        (incoming_terms, micro_cols, moved)
    )
    packed_of = dict(enumerate(moved))
    packed_of[last_section] = packed
    every_slot = incoming_terms[:, 0, :, chunk].astype(jnp.int32)
    onehot = (every_slot[:, :, None] == jnp.arange(block_total, dtype=jnp.int32)).astype(
        jnp.bfloat16
    )
    dense = jnp.einsum(
        "qsfc,qfn->snc", incoming_terms[:, :, :, :chunk], onehot, preferred_element_type=jnp.float32
    )
    dense = dense.reshape(stripe, block_total, chunk).astype(jnp.bfloat16)
    passage_out = gathered_columns(dense.reshape(stripe * block_total, chunk), "section")
    passage_out = passage_out.reshape(stripe, block_total, width)
    entry = lax.all_to_all(carry_start, "dp", split_axis=0, concat_axis=1, tiled=True)
    section_index = lax.axis_index("section")
    last = section_count - 1
    carry = entry.reshape(dp_count * micro_count, col_width)
    sent_of = {}
    for source in range(last, -1, -1):
        rows = packed_of[source][:col_width]
        pre = packed_of[source][col_width].astype(jnp.float32)
        sigma = jax.nn.sigmoid(pre)
        slope = sigma * (1.0 + pre * (1.0 - sigma))
        inner = (carry * slope).astype(jnp.bfloat16)
        piece = gathered_pieces(inner, "dp")
        back_sum = jnp.einsum("dmj,idj->mi", piece, rows, preferred_element_type=jnp.float32)
        carry = carry + back_sum
        if source == last:
            grad_cols, home_inner = (carry, inner)
        else:
            both = jnp.stack([carry, inner.astype(jnp.float32)])
            sent_of[source] = lax.ppermute(both, "section", [(last, source)])
    for source in range(last):
        here = section_index == source
        grad_cols = jnp.where(here, sent_of[source][0], grad_cols)
        home_inner = jnp.where(here, sent_of[source][1].astype(jnp.bfloat16), home_inner)
    home_piece = gathered_pieces(home_inner, "dp")
    grad_weight = (
        jnp.einsum("mi,dmj->idj", section_inputs[0], home_piece, preferred_element_type=jnp.float32)
        .reshape(col_width, width)
        .astype(jnp.bfloat16)
    )
    return (
        query_sums.reshape(blocks_here * row_block_count, width).astype(jnp.bfloat16),
        passage_out,
        grad_cols[None],
        grad_weight[None],
    )


def solution(mesh):
    placed = (
        P(("section", "dp"), None),
        P("dp", None, None),
        P("section", None),
        P("section"),
        P(("section", "dp"), None),
        P("section", "dp", None),
        P("section", None, "dp"),
        P("section", None, "dp"),
    )
    return jax.shard_map(
        body,
        mesh=mesh,
        in_specs=placed,
        out_specs=(
            P(("section", "dp"), None),
            P("dp", None, None),
            P("section", None, "dp"),
            P("section", "dp", None),
        ),
        check_vma=False,
    )
```

profile of v0, /device:TPU:1, one launch (start us, length us, event | category | flops | bytes accessed | tf_op | source)
XLA Modules:
  0.0 601.3 jit_solution(9847557009770879357)
XLA Ops:
  1.6 2.1 fusion.1
  3.7 4.4 copy.128
  8.1 15.1 %all-to-all-start = ((bf16[2,192,3584]{2,0,1:T(2,128)(2,1)}), bf16[2,192,3584]{2,0,1:T(2,128)(2,1)}, u32[]{:S(2)}, u32[]{:S(2)}) async-start(bf16[2,192,3584]{2,0,1:T(2,128)(2,1)} %copy.128), calls=%async_computation | async-start | bytes 5505024 | tf_op jit(solution)/shard_map/all_to_all | solution.py:50
  25.1 63.2 %all-to-all-done = bf16[2,192,3584]{2,0,1:T(2,128)(2,1)} async-done(((bf16[2,192,3584]{2,0,1:T(2,128)(2,1)}), bf16[2,192,3584]{2,0,1:T(2,128)(2,1)}, u32[]{:S(2)}, u32[]{:S(2)}) %all-to-all-start) | async-done | bytes 2752544 | tf_op jit(solution)/shard_map/all_to_all | solution.py:50
  88.3 5.2 copy.129
  93.5 6.8 %reshape.247 = bf16[128,3,3584]{2,0,1:T(8,128)(2,1)} reshape(bf16[64,2,3,3584]{3,1,0,2:T(2,128)(2,1)} %copy.129) | data formatting | bytes 5505024 | tf_op jit(solution)/shard_map/reshape.5
  100.2 2.7 fusion.37
  103.2 2.4 fusion.2
  105.7 6.8 %convert_element_type.163 = bf16[64,2,3,8,448]{4,3,1,0,2:T(8,128)(2,1)} reshape(bf16[128,1,3,3584]{3,0,2,1:T(8,128)(2,1)} %fusion.2) | data formatting | bytes 5505024 | tf_op jit(solution)/shard_map/convert_element_type | solution.py:91
  112.4 3.6 copy.132
  116.8 4.9 copy.133
  121.7 14.9 %all-to-all-start.1 = ((bf16[512,2,3,449]{3,1,2,0:T(2,128)(2,1)}), bf16[512,2,3,449]{3,1,2,0:T(2,128)(2,1)}, u32[]{:S(2)}, u32[]{:S(2)}) async-start(bf16[512,2,3,449]{3,1,2,0:T(2,128)(2,1)} %copy.133), calls=%async_computation.1 | async-start | bytes 6291456 | tf_op jit(solution)/shard_map/all_to_all | solution.py:99
  136.6 1.9 reshape_squeeze.3
  139.3 4.9 collective-permute-start
  144.9 1.6 collective-permute-start.2
  146.5 1.5 collective-permute-start.3
  148.0 1.6 collective-permute-start.4
  149.6 117.1 %collective-permute-done = bf16[57,64,56]{1,2,0:T(8,128)(2,1)S(1)} collective-permute-done((bf16[57,64,56]{1,2,0:T(8,128)(2,1)S(1)}, bf16[57,64,56]{1,2,0:T(8,128)(2,1)S(1)}, u32[]{:S(2)}, u32[]{:S(2)}) %collective-permute-start) | collective-permute-done | bytes 408608 | tf_op jit(solution)/shard_map/ppermute | solution.py:108
  266.7 1.6 collective-permute-start.5
  269.2 1.5 collective-permute-start.6
  270.7 3.4 fusion.124
  274.2 23.9 %all_to_all.79 = f32[64,1,56]{2,1,0:T(1,128)S(1)} all-to-all(f32[64,1,56]{2,1,0:T(1,128)S(1)} %bitcast.302), channel_id=1, replica_groups=mesh['section'=8,'dp'=64] {'dp'}, dimensions={0} | all-to-all | bytes 28672 | tf_op jit(solution)/shard_map/all_to_all | solution.py:127
  299.6 19.9 %all_to_all.80 = bf16[64,2,1792]{2,1,0:T(2,128)(2,1)S(1)} all-to-all(bf16[64,2,1792]{2,1,0:T(2,128)(2,1)S(1)} %reshape.284), channel_id=1, replica_groups=mesh['section'=8,'dp'=64] {'dp'}, dimensions={0} | all-to-all | bytes 917504 | tf_op jit(solution)/shard_map/all_to_all | solution.py:18
  320.0 2.2 bitcast_convert_fusion.6
  322.3 1.3 reshape.286
  323.7 6.3 %all-to-all-start.5 = ((bf16[64,2,1792]{2,1,0:T(2,128)(2,1)}), bf16[64,2,1792]{2,1,0:T(2,128)(2,1)S(1)}, u32[]{:S(2)}, u32[]{:S(2)}) async-start(bf16[64,2,1792]{2,1,0:T(2,128)(2,1)} %reshape.286), calls=%async_computation.5 | async-start | bytes 917504 | tf_op jit(solution)/shard_map/all_to_all | solution.py:18
  331.2 2.2 copy.143
  333.4 12.5 %all-to-all-done.5 = bf16[64,2,1792]{2,1,0:T(2,128)(2,1)S(1)} async-done(((bf16[64,2,1792]{2,1,0:T(2,128)(2,1)}), bf16[64,2,1792]{2,1,0:T(2,128)(2,1)S(1)}, u32[]{:S(2)}, u32[]{:S(2)}) %all-to-all-start.5) | async-done | bytes 458784 | tf_op jit(solution)/shard_map/all_to_all | solution.py:18
  346.5 1.8 bitcast_convert_fusion.5
  348.4 1.3 reshape.288
  349.7 6.3 %all-to-all-start.6 = ((bf16[64,2,1792]{2,1,0:T(2,128)(2,1)}), bf16[64,2,1792]{2,1,0:T(2,128)(2,1)S(1)}, u32[]{:S(2)}, u32[]{:S(2)}) async-start(bf16[64,2,1792]{2,1,0:T(2,128)(2,1)} %reshape.288), calls=%async_computation.6 | async-start | bytes 917504 | tf_op jit(solution)/shard_map/all_to_all | solution.py:18
  357.2 2.2 copy.144
  359.4 12.5 %all-to-all-done.6 = bf16[64,2,1792]{2,1,0:T(2,128)(2,1)S(1)} async-done(((bf16[64,2,1792]{2,1,0:T(2,128)(2,1)}), bf16[64,2,1792]{2,1,0:T(2,128)(2,1)S(1)}, u32[]{:S(2)}, u32[]{:S(2)}) %all-to-all-start.6) | async-done | bytes 458784 | tf_op jit(solution)/shard_map/all_to_all | solution.py:18
  372.5 1.8 bitcast_convert_fusion.4
  375.7 6.3 %all-to-all-start.7 = ((bf16[64,2,1792]{2,1,0:T(2,128)(2,1)}), bf16[64,2,1792]{2,1,0:T(2,128)(2,1)S(1)}, u32[]{:S(2)}, u32[]{:S(2)}) async-start(bf16[64,2,1792]{2,1,0:T(2,128)(2,1)} %reshape.290), calls=%async_computation.7 | async-start | bytes 917504 | tf_op jit(solution)/shard_map/all_to_all | solution.py:18
  383.2 2.2 copy.145
  385.4 12.5 %all-to-all-done.7 = bf16[64,2,1792]{2,1,0:T(2,128)(2,1)S(1)} async-done(((bf16[64,2,1792]{2,1,0:T(2,128)(2,1)}), bf16[64,2,1792]{2,1,0:T(2,128)(2,1)S(1)}, u32[]{:S(2)}, u32[]{:S(2)}) %all-to-all-start.7) | async-done | bytes 458784 | tf_op jit(solution)/shard_map/all_to_all | solution.py:18
  398.4 1.7 bitcast_convert_fusion.3
  401.7 6.3 %all-to-all-start.8 = ((bf16[64,2,1792]{2,1,0:T(2,128)(2,1)}), bf16[64,2,1792]{2,1,0:T(2,128)(2,1)S(1)}, u32[]{:S(2)}, u32[]{:S(2)}) async-start(bf16[64,2,1792]{2,1,0:T(2,128)(2,1)} %reshape.292), calls=%async_computation.8 | async-start | bytes 917504 | tf_op jit(solution)/shard_map/all_to_all | solution.py:18
  409.2 2.2 copy.146
  411.4 12.5 %all-to-all-done.8 = bf16[64,2,1792]{2,1,0:T(2,128)(2,1)S(1)} async-done(((bf16[64,2,1792]{2,1,0:T(2,128)(2,1)}), bf16[64,2,1792]{2,1,0:T(2,128)(2,1)S(1)}, u32[]{:S(2)}, u32[]{:S(2)}) %all-to-all-start.8) | async-done | bytes 458784 | tf_op jit(solution)/shard_map/all_to_all | solution.py:18
  424.4 1.8 bitcast_convert_fusion.2
  427.6 6.3 %all-to-all-start.9 = ((bf16[64,2,1792]{2,1,0:T(2,128)(2,1)}), bf16[64,2,1792]{2,1,0:T(2,128)(2,1)S(1)}, u32[]{:S(2)}, u32[]{:S(2)}) async-start(bf16[64,2,1792]{2,1,0:T(2,128)(2,1)} %reshape.294), calls=%async_computation.9 | async-start | bytes 917504 | tf_op jit(solution)/shard_map/all_to_all | solution.py:18
  435.1 2.2 copy.147
  437.3 12.5 %all-to-all-done.9 = bf16[64,2,1792]{2,1,0:T(2,128)(2,1)S(1)} async-done(((bf16[64,2,1792]{2,1,0:T(2,128)(2,1)}), bf16[64,2,1792]{2,1,0:T(2,128)(2,1)S(1)}, u32[]{:S(2)}, u32[]{:S(2)}) %all-to-all-start.9) | async-done | bytes 458784 | tf_op jit(solution)/shard_map/all_to_all | solution.py:18
  450.4 1.7 bitcast_convert_fusion.1
  453.6 6.6 %all-to-all-start.10 = ((bf16[64,2,1792]{2,1,0:T(2,128)(2,1)}), bf16[64,2,1792]{2,1,0:T(2,128)(2,1)S(1)}, u32[]{:S(2)}, u32[]{:S(2)}) async-start(bf16[64,2,1792]{2,1,0:T(2,128)(2,1)} %reshape.296), calls=%async_computation.10 | async-start | bytes 917504 | tf_op jit(solution)/shard_map/all_to_all | solution.py:18
  461.4 2.2 copy.148
  463.6 12.4 %all-to-all-done.10 = bf16[64,2,1792]{2,1,0:T(2,128)(2,1)S(1)} async-done(((bf16[64,2,1792]{2,1,0:T(2,128)(2,1)}), bf16[64,2,1792]{2,1,0:T(2,128)(2,1)S(1)}, u32[]{:S(2)}, u32[]{:S(2)}) %all-to-all-start.10) | async-done | bytes 458784 | tf_op jit(solution)/shard_map/all_to_all | solution.py:18
  477.7 1.3 reshape.298
  479.0 6.3 %all-to-all-start.11 = ((bf16[64,2,1792]{2,1,0:T(2,128)(2,1)}), bf16[64,2,1792]{2,1,0:T(2,128)(2,1)S(1)}, u32[]{:S(2)}, u32[]{:S(2)}) async-start(bf16[64,2,1792]{2,1,0:T(2,128)(2,1)} %reshape.298), calls=%async_computation.11 | async-start | bytes 917504 | tf_op jit(solution)/shard_map/all_to_all | solution.py:18
  485.3 8.7 %copy.135 = bf16[512,2,3,449]{0,3,2,1:T(8,128)(2,1)} copy(bf16[512,2,3,449]{3,1,2,0:T(2,128)(2,1)} %all-to-all-done.1) | data formatting | bytes 5517312 | tf_op jit(solution)/shard_map/optimization_barrier | solution.py:112
  494.8 2.7 fusion.10
  497.6 3.6 all-to-all-done.11
  502.4 37.4 %all-to-all-start.2 = ((bf16[8,128,448]{1,2,0:T(8,128)(2,1)}), bf16[8,128,448]{1,2,0:T(8,128)(2,1)S(1)}, u32[]{:S(2)}, u32[]{:S(2)}) async-start(bf16[8,128,448]{1,2,0:T(8,128)(2,1)} %broadcast_in_dim.137), calls=%async_computation.2 | async-start | bytes 1835008 | tf_op jit(solution)/shard_map/all_to_all | solution.py:24
  539.9 2.2 copy.149
  553.5 13.6 %collective-permute-done.13 = f32[2,64,56]{1,2,0:T(8,128)S(1)} collective-permute-done((f32[2,64,56]{1,2,0:T(8,128)S(1)}, f32[2,64,56]{1,2,0:T(8,128)S(1)}, u32[]{:S(2)}, u32[]{:S(2)}) %collective-permute-start.13) | collective-permute-done | bytes 28704 | tf_op jit(solution)/shard_map/ppermute | solution.py:145
  568.0 1.3 reshape.300
  569.3 10.5 %all-to-all-start.12 = ((bf16[64,2,1792]{2,1,0:T(2,128)(2,1)}), bf16[64,2,1792]{2,1,0:T(2,128)(2,1)S(1)}, u32[]{:S(2)}, u32[]{:S(2)}) async-start(bf16[64,2,1792]{2,1,0:T(2,128)(2,1)} %reshape.300), calls=%async_computation.12 | async-start | bytes 917504 | tf_op jit(solution)/shard_map/all_to_all | solution.py:18
  580.9 2.1 reshape_reshape.3
  583.0 1.5 fusion.107
  584.5 11.1 %all-to-all-done.12 = bf16[64,2,1792]{2,1,0:T(2,128)(2,1)S(1)} async-done(((bf16[64,2,1792]{2,1,0:T(2,128)(2,1)}), bf16[64,2,1792]{2,1,0:T(2,128)(2,1)S(1)}, u32[]{:S(2)}, u32[]{:S(2)}) %all-to-all-start.12) | async-done | bytes 458784 | tf_op jit(solution)/shard_map/all_to_all | solution.py:18
  597.1 1.4 copy.151
  598.5 2.5 convert_element_type.195
  (141 shorter events, 42.7 us)
Async XLA Ops:
  0.6 99.6 %copy-start = (bf16[128,3584]{1,0:T(8,128)(2,1)S(1)}, bf16[128,3584]{1,0:T(8,128)(2,1)}, u32[]{:S(2)}) copy-start(bf16[128,3584]{1,0:T(8,128)(2,1)} %param.8) | copy-start | bytes 2752516
  8.1 15.2 %copy-start.11 = (f32[128,384]{1,0:T(8,128)S(1)}, f32[128,384]{1,0:T(8,128)}, u32[]{:S(2)}) copy-start(f32[128,384]{1,0:T(8,128)} %param.12) | copy-start | bytes 589828
  8.1 15.3 %copy-start.26 = (s32[64]{0:T(128)S(1)}, s32[64]{0:T(128)}, u32[]{:S(2)}) copy-start(s32[64]{0:T(128)} %param.11) | copy-start | bytes 772
  8.1 80.2 %all-to-all-start = ((bf16[2,192,3584]{2,0,1:T(2,128)(2,1)}), bf16[2,192,3584]{2,0,1:T(2,128)(2,1)}, u32[]{:S(2)}, u32[]{:S(2)}) async-start(bf16[2,192,3584]{2,0,1:T(2,128)(2,1)} %copy.128), calls=%async_computation | async-start | bytes 5505024 | tf_op jit(solution)/shard_map/all_to_all | solution.py:50
  121.7 14.9 %copy-start.5 = (bf16[1,56,3584]{2,1,0:T(8,128)(2,1)S(1)}, bf16[1,56,3584]{2,1,0:T(8,128)(2,1)}, u32[]{:S(2)}) copy-start(bf16[1,56,3584]{2,1,0:T(8,128)(2,1)} %param.13) | copy-start | bytes 1204228
  121.7 152.5 %all-to-all-start.1 = ((bf16[512,2,3,449]{3,1,2,0:T(2,128)(2,1)}), bf16[512,2,3,449]{3,1,2,0:T(2,128)(2,1)}, u32[]{:S(2)}, u32[]{:S(2)}) async-start(bf16[512,2,3,449]{3,1,2,0:T(2,128)(2,1)} %copy.133), calls=%async_computation.1 | async-start | bytes 6291456 | tf_op jit(solution)/shard_map/all_to_all | solution.py:99
  136.6 2.5 copy-start.22
  139.3 127.4 %collective-permute-start = (bf16[57,64,56]{1,2,0:T(8,128)(2,1)S(1)}, bf16[57,64,56]{1,2,0:T(8,128)(2,1)S(1)}, u32[]{:S(2)}, u32[]{:S(2)}) collective-permute-start(bf16[57,64,56]{1,2,0:T(8,128)(2,1)S(1)} %pad_maximum_fusion.1), channel_id=1, source_target_pairs={{0,448},{1,449},{2,450},{3,451},{4,452},{5,453},{6,454},{7,455},{8... | collective-permute-start | bytes 1225736 | tf_op jit(solution)/shard_map/ppermute | solution.py:108
  144.2 124.1 %collective-permute-start.1 = (bf16[57,64,56]{1,2,0:T(8,128)(2,1)S(1)}, bf16[57,64,56]{1,2,0:T(8,128)(2,1)S(1)}, u32[]{:S(2)}, u32[]{:S(2)}) collective-permute-start(bf16[57,64,56]{1,2,0:T(8,128)(2,1)S(1)} %pad_maximum_fusion.1), channel_id=1, source_target_pairs={{64,448},{65,449},{66,450},{67,451},{68,452},{69,453},{70,454},{71... | collective-permute-start | bytes 1225736 | tf_op jit(solution)/shard_map/ppermute | solution.py:108
  144.9 129.3 %collective-permute-start.2 = (bf16[57,64,56]{1,2,0:T(8,128)(2,1)S(1)}, bf16[57,64,56]{1,2,0:T(8,128)(2,1)}, u32[]{:S(2)}, u32[]{:S(2)}) collective-permute-start(bf16[57,64,56]{1,2,0:T(8,128)(2,1)S(1)} %pad_maximum_fusion.1), channel_id=1, source_target_pairs={{128,448},{129,449},{130,450},{131,451},{132,452},{133,453},{134,4... | collective-permute-start | bytes 1225736 | tf_op jit(solution)/shard_map/ppermute | solution.py:108
  146.5 127.7 %collective-permute-start.3 = (bf16[57,64,56]{1,2,0:T(8,128)(2,1)S(1)}, bf16[57,64,56]{1,2,0:T(8,128)(2,1)}, u32[]{:S(2)}, u32[]{:S(2)}) collective-permute-start(bf16[57,64,56]{1,2,0:T(8,128)(2,1)S(1)} %pad_maximum_fusion.1), channel_id=1, source_target_pairs={{192,448},{193,449},{194,450},{195,451},{196,452},{197,453},{198,4... | collective-permute-start | bytes 1225736 | tf_op jit(solution)/shard_map/ppermute | solution.py:108
  148.0 126.2 %collective-permute-start.4 = (bf16[57,64,56]{1,2,0:T(8,128)(2,1)S(1)}, bf16[57,64,56]{1,2,0:T(8,128)(2,1)}, u32[]{:S(2)}, u32[]{:S(2)}) collective-permute-start(bf16[57,64,56]{1,2,0:T(8,128)(2,1)S(1)} %pad_maximum_fusion.1), channel_id=1, source_target_pairs={{256,448},{257,449},{258,450},{259,451},{260,452},{261,453},{262,4... | collective-permute-start | bytes 1225736 | tf_op jit(solution)/shard_map/ppermute | solution.py:108
  266.7 209.8 %copy-start.2 = (bf16[57,64,56]{1,2,0:T(8,128)(2,1)}, bf16[57,64,56]{1,2,0:T(8,128)(2,1)S(1)}, u32[]{:S(2)}) copy-start(bf16[57,64,56]{1,2,0:T(8,128)(2,1)S(1)} %collective-permute-done) | copy-start | bytes 1225732
  266.7 7.5 %collective-permute-start.5 = (bf16[57,64,56]{1,2,0:T(8,128)(2,1)S(1)}, bf16[57,64,56]{1,2,0:T(8,128)(2,1)}, u32[]{:S(2)}, u32[]{:S(2)}) collective-permute-start(bf16[57,64,56]{1,2,0:T(8,128)(2,1)S(1)} %pad_maximum_fusion.1), channel_id=1, source_target_pairs={{320,448},{321,449},{322,450},{323,451},{324,452},{325,453},{326,4... | collective-permute-start | bytes 1225736 | tf_op jit(solution)/shard_map/ppermute | solution.py:108
  268.3 0.9 copy-start.4
  269.2 5.1 collective-permute-start.6
  298.3 0.6 copy-start.12
  322.2 24.3 %copy-start.20 = (f32[64,56]{0,1:T(8,128)}, f32[64,56]{0,1:T(8,128)S(1)}, u32[]{:S(2)}) copy-start(f32[64,56]{0,1:T(8,128)S(1)} %get-tuple-element.40) | copy-start | bytes 43012
  323.7 22.3 %all-to-all-start.5 = ((bf16[64,2,1792]{2,1,0:T(2,128)(2,1)}), bf16[64,2,1792]{2,1,0:T(2,128)(2,1)S(1)}, u32[]{:S(2)}, u32[]{:S(2)}) async-start(bf16[64,2,1792]{2,1,0:T(2,128)(2,1)} %reshape.286), calls=%async_computation.5 | async-start | bytes 917504 | tf_op jit(solution)/shard_map/all_to_all | solution.py:18
  349.7 22.2 %all-to-all-start.6 = ((bf16[64,2,1792]{2,1,0:T(2,128)(2,1)}), bf16[64,2,1792]{2,1,0:T(2,128)(2,1)S(1)}, u32[]{:S(2)}, u32[]{:S(2)}) async-start(bf16[64,2,1792]{2,1,0:T(2,128)(2,1)} %reshape.288), calls=%async_computation.6 | async-start | bytes 917504 | tf_op jit(solution)/shard_map/all_to_all | solution.py:18
  375.7 22.2 %all-to-all-start.7 = ((bf16[64,2,1792]{2,1,0:T(2,128)(2,1)}), bf16[64,2,1792]{2,1,0:T(2,128)(2,1)S(1)}, u32[]{:S(2)}, u32[]{:S(2)}) async-start(bf16[64,2,1792]{2,1,0:T(2,128)(2,1)} %reshape.290), calls=%async_computation.7 | async-start | bytes 917504 | tf_op jit(solution)/shard_map/all_to_all | solution.py:18
  401.7 22.2 %all-to-all-start.8 = ((bf16[64,2,1792]{2,1,0:T(2,128)(2,1)}), bf16[64,2,1792]{2,1,0:T(2,128)(2,1)S(1)}, u32[]{:S(2)}, u32[]{:S(2)}) async-start(bf16[64,2,1792]{2,1,0:T(2,128)(2,1)} %reshape.292), calls=%async_computation.8 | async-start | bytes 917504 | tf_op jit(solution)/shard_map/all_to_all | solution.py:18
  426.2 24.2 %copy-start.6 = (f32[64,56]{0,1:T(8,128)}, f32[64,56]{0,1:T(8,128)S(1)}, u32[]{:S(2)}) copy-start(f32[64,56]{0,1:T(8,128)S(1)} %get-tuple-element.44) | copy-start | bytes 43012
  427.6 22.2 %all-to-all-start.9 = ((bf16[64,2,1792]{2,1,0:T(2,128)(2,1)}), bf16[64,2,1792]{2,1,0:T(2,128)(2,1)S(1)}, u32[]{:S(2)}, u32[]{:S(2)}) async-start(bf16[64,2,1792]{2,1,0:T(2,128)(2,1)} %reshape.294), calls=%async_computation.9 | async-start | bytes 917504 | tf_op jit(solution)/shard_map/all_to_all | solution.py:18
  452.1 24.4 %copy-start.8 = (f32[64,56]{0,1:T(8,128)}, f32[64,56]{0,1:T(8,128)S(1)}, u32[]{:S(2)}) copy-start(f32[64,56]{0,1:T(8,128)S(1)} %get-tuple-element.45) | copy-start | bytes 43012
  453.6 22.4 %all-to-all-start.10 = ((bf16[64,2,1792]{2,1,0:T(2,128)(2,1)}), bf16[64,2,1792]{2,1,0:T(2,128)(2,1)S(1)}, u32[]{:S(2)}, u32[]{:S(2)}) async-start(bf16[64,2,1792]{2,1,0:T(2,128)(2,1)} %reshape.296), calls=%async_computation.10 | async-start | bytes 917504 | tf_op jit(solution)/shard_map/all_to_all | solution.py:18
  479.0 22.2 %all-to-all-start.11 = ((bf16[64,2,1792]{2,1,0:T(2,128)(2,1)}), bf16[64,2,1792]{2,1,0:T(2,128)(2,1)S(1)}, u32[]{:S(2)}, u32[]{:S(2)}) async-start(bf16[64,2,1792]{2,1,0:T(2,128)(2,1)} %reshape.298), calls=%async_computation.11 | async-start | bytes 917504 | tf_op jit(solution)/shard_map/all_to_all | solution.py:18
  494.8 45.0 %copy-start.3 = (bf16[57,64,56]{1,2,0:T(8,128)(2,1)S(1)}, bf16[57,64,56]{1,2,0:T(8,128)(2,1)}, u32[]{:S(2)}) copy-start(bf16[57,64,56]{1,2,0:T(8,128)(2,1)} %copy-done.2) | copy-start | bytes 1225732
  502.3 39.8 %copy-start.24 = (f32[1,64,56]{1,2,0:T(8,128)S(1)}, f32[1,64,56]{1,2,0:T(8,128)}, u32[]{:S(2)}) copy-start(f32[1,64,56]{1,2,0:T(8,128)} %get-tuple-element.22) | copy-start | bytes 43012
  502.3 41.7 %copy-start.14 = (f32[1,64,56]{1,2,0:T(8,128)S(1)}, f32[1,64,56]{1,2,0:T(8,128)}, u32[]{:S(2)}) copy-start(f32[1,64,56]{1,2,0:T(8,128)} %get-tuple-element.24) | copy-start | bytes 43012
  502.3 43.6 %copy-start.15 = (f32[1,64,56]{1,2,0:T(8,128)S(1)}, f32[1,64,56]{1,2,0:T(8,128)}, u32[]{:S(2)}) copy-start(f32[1,64,56]{1,2,0:T(8,128)} %get-tuple-element.26) | copy-start | bytes 43012
  502.3 44.9 %copy-start.7 = (f32[64,56]{0,1:T(8,128)S(1)}, f32[64,56]{0,1:T(8,128)}, u32[]{:S(2)}) copy-start(f32[64,56]{0,1:T(8,128)} %copy-done.6) | copy-start | bytes 43012
  502.3 44.9 %copy-start.16 = (f32[1,64,56]{1,2,0:T(8,128)S(1)}, f32[1,64,56]{1,2,0:T(8,128)}, u32[]{:S(2)}) copy-start(f32[1,64,56]{1,2,0:T(8,128)} %get-tuple-element.28) | copy-start | bytes 43012
  502.3 46.1 %copy-start.9 = (f32[64,56]{0,1:T(8,128)S(1)}, f32[64,56]{0,1:T(8,128)}, u32[]{:S(2)}) copy-start(f32[64,56]{0,1:T(8,128)} %copy-done.8) | copy-start | bytes 43012
  502.3 46.1 %copy-start.17 = (f32[1,64,56]{1,2,0:T(8,128)S(1)}, f32[1,64,56]{1,2,0:T(8,128)}, u32[]{:S(2)}) copy-start(f32[1,64,56]{1,2,0:T(8,128)} %get-tuple-element.30) | copy-start | bytes 43012
  502.3 47.4 %copy-start.10 = (f32[64,56]{0,1:T(8,128)S(1)}, f32[64,56]{0,1:T(8,128)}, u32[]{:S(2)}) copy-start(f32[64,56]{0,1:T(8,128)} %get-tuple-element.46) | copy-start | bytes 43012
  502.3 47.4 %copy-start.18 = (f32[1,64,56]{1,2,0:T(8,128)S(1)}, f32[1,64,56]{1,2,0:T(8,128)}, u32[]{:S(2)}) copy-start(f32[1,64,56]{1,2,0:T(8,128)} %get-tuple-element.32) | copy-start | bytes 43012
  502.4 67.0 %all-to-all-start.2 = ((bf16[8,128,448]{1,2,0:T(8,128)(2,1)}), bf16[8,128,448]{1,2,0:T(8,128)(2,1)S(1)}, u32[]{:S(2)}, u32[]{:S(2)}) async-start(bf16[8,128,448]{1,2,0:T(8,128)(2,1)} %broadcast_in_dim.137), calls=%async_computation.2 | async-start | bytes 1835008 | tf_op jit(solution)/shard_map/all_to_all | solution.py:24
  539.8 11.5 %copy-start.19 = (f32[1,64,56]{1,2,0:T(8,128)S(1)}, f32[1,64,56]{1,2,0:T(8,128)}, u32[]{:S(2)}) copy-start(f32[1,64,56]{1,2,0:T(8,128)} %get-tuple-element.34) | copy-start | bytes 43012
  539.9 27.2 %copy-start.13 = (bf16[1,64,56]{1,2,0:T(8,128)(2,1)S(1)}, bf16[1,64,56]{1,2,0:T(8,128)(2,1)}, u32[]{:S(2)}) copy-start(bf16[1,64,56]{1,2,0:T(8,128)(2,1)} %copy-done.12) | copy-start | bytes 21508
  542.7 8.7 %collective-permute-start.7 = (f32[2,64,56]{1,2,0:T(8,128)}, f32[2,64,56]{1,2,0:T(8,128)}, u32[]{:S(2)}, u32[]{:S(2)}) collective-permute-start(f32[2,64,56]{1,2,0:T(8,128)} %pad_maximum_fusion.2), channel_id=1, source_target_pairs={{448,384},{449,385},{450,386},{451,387},{452,388},{453,389},{454,3... | collective-permute-start | bytes 86024 | tf_op jit(solution)/shard_map/ppermute | solution.py:145
  544.6 7.5 %collective-permute-start.8 = (f32[2,64,56]{1,2,0:T(8,128)}, f32[2,64,56]{1,2,0:T(8,128)}, u32[]{:S(2)}, u32[]{:S(2)}) collective-permute-start(f32[2,64,56]{1,2,0:T(8,128)} %pad_maximum_fusion.3), channel_id=1, source_target_pairs={{448,320},{449,321},{450,322},{451,323},{452,324},{453,325},{454,3... | collective-permute-start | bytes 86024 | tf_op jit(solution)/shard_map/ppermute | solution.py:145
  545.9 7.5 %collective-permute-start.9 = (f32[2,64,56]{1,2,0:T(8,128)S(1)}, f32[2,64,56]{1,2,0:T(8,128)}, u32[]{:S(2)}, u32[]{:S(2)}) collective-permute-start(f32[2,64,56]{1,2,0:T(8,128)S(1)} %pad_maximum_fusion.4), channel_id=1, source_target_pairs={{448,256},{449,257},{450,258},{451,259},{452,260},{453,261},{454,2... | collective-permute-start | bytes 86024 | tf_op jit(solution)/shard_map/ppermute | solution.py:145
  547.2 6.3 %collective-permute-start.10 = (f32[2,64,56]{1,2,0:T(8,128)S(1)}, f32[2,64,56]{1,2,0:T(8,128)}, u32[]{:S(2)}, u32[]{:S(2)}) collective-permute-start(f32[2,64,56]{1,2,0:T(8,128)S(1)} %pad_maximum_fusion.5), channel_id=1, source_target_pairs={{448,192},{449,193},{450,194},{451,195},{452,196},{453,197},{454,1... | collective-permute-start | bytes 86024 | tf_op jit(solution)/shard_map/ppermute | solution.py:145
  548.5 5.0 collective-permute-start.11
  550.4 1.0 copy-start.23
  551.4 2.0 collective-permute-start.12
  552.1 14.9 %collective-permute-start.13 = (f32[2,64,56]{1,2,0:T(8,128)S(1)}, f32[2,64,56]{1,2,0:T(8,128)S(1)}, u32[]{:S(2)}, u32[]{:S(2)}) collective-permute-start(f32[2,64,56]{1,2,0:T(8,128)S(1)} %pad_maximum_fusion.8), channel_id=1, source_target_pairs={{448,0},{449,1},{450,2},{451,3},{452,4},{453,5},{454,6},{455,7},{4... | collective-permute-start | bytes 86024 | tf_op jit(solution)/shard_map/ppermute | solution.py:145
  569.3 13.6 %copy-start.21 = (f32[64,56]{0,1:T(8,128)S(1)}, f32[64,56]{0,1:T(8,128)}, u32[]{:S(2)}) copy-start(f32[64,56]{0,1:T(8,128)} %copy-done.20) | copy-start | bytes 43012
  569.3 26.3 %all-to-all-start.12 = ((bf16[64,2,1792]{2,1,0:T(2,128)(2,1)}), bf16[64,2,1792]{2,1,0:T(2,128)(2,1)S(1)}, u32[]{:S(2)}, u32[]{:S(2)}) async-start(bf16[64,2,1792]{2,1,0:T(2,128)(2,1)} %reshape.300), calls=%async_computation.12 | async-start | bytes 917504 | tf_op jit(solution)/shard_map/all_to_all | solution.py:18
  579.8 16.3 %copy-start.25 = (bf16[1,64,56]{1,2,0:T(8,128)(2,1)S(1)}, bf16[1,64,56]{1,2,0:T(8,128)(2,1)}, u32[]{:S(2)}) copy-start(bf16[1,64,56]{1,2,0:T(8,128)(2,1)} %param.14) | copy-start | bytes 21508
  583.0 18.1 %copy-start.1 = (bf16[128,3584]{1,0:T(8,128)(2,1)S(1)}, bf16[128,3584]{1,0:T(8,128)(2,1)}, u32[]{:S(2)}) copy-start(bf16[128,3584]{1,0:T(8,128)(2,1)} %param.8) | copy-start | bytes 2752516
where the time goes:
time: 612 us; the launch traced here: 601 us
  waiting for transfers between devices  284 us (46%)
  starting transfers between devices  144 us (24%)
  local copies, waits for them, and re-layouts  94.4 us (15%)
  blocking collectives  43.8 us (7%)
  matrix products  26.7 us (4%)
  other arithmetic  7.1 us (1%)
    ppermute x7, waiting for transfers between devices, body(): lax.ppermute(packed, 'section', [(source, last_section)])  117 us
    all_to_all x8, waiting for transfers between devices, gathered_pieces(): return lax.all_to_all(copies, axis, 0, 0, tiled=True)  89.7 us
    all_to_all x1, waiting for transfers between devices, body(): lax.all_to_all(outgoing, 'dp', split_axis=1, concat_axis=0, tiled=True)  63.2 us
    all_to_all x8, starting transfers between devices, gathered_pieces(): return lax.all_to_all(copies, axis, 0, 0, tiled=True)  54.8 us
    all_to_all x1, starting transfers between devices, gathered_columns(): pieces = lax.all_to_all(copies, axis, 0, 0, tiled=True)  37.4 us
    all_to_all x1, blocking collectives, body(): lax.all_to_all(carry_start, 'dp', split_axis=0, concat_axis=1, tiled=True)  23.9 us
    slice x14, local copies, waits for them, and re-layouts, body(): rows = packed_of[source][:col_width]  22.6 us
    all_to_all x1, blocking collectives, gathered_pieces(): return lax.all_to_all(copies, axis, 0, 0, tiled=True)  19.9 us
  transfers between devices with their start and end apart: 25, of which 11 were waited for; matrix products, arithmetic and copies ran while one was open for 9% of the time, Pallas kernels for 0%

commit v1 on v0

--- a/solution.py
+++ b/solution.py
@@ -124,7 +124,10 @@
     dense = dense.reshape(stripe, block_total, chunk).astype(jnp.bfloat16)
     passage_out = gathered_columns(dense.reshape(stripe * block_total, chunk), "section")
     passage_out = passage_out.reshape(stripe, block_total, width)
-    entry = lax.all_to_all(carry_start, "dp", split_axis=0, concat_axis=1, tiled=True)
+    entry = jnp.concatenate(
+        lax.all_to_all(jnp.stack(jnp.split(carry_start, lax.axis_size("dp"), axis=0)), "dp", 0, 0),
+        axis=1,
+    )
     section_index = lax.axis_index("section")
     last = section_count - 1
     carry = entry.reshape(dp_count * micro_count, col_width)

time: 612 us -> 613 us (level)
    unnamed x84 -> x147, local copies, waits for them, and re-layouts: 19.7 us -> 20.3 us
where the time goes in v1:
time: 613 us; the launch traced here: 602 us
  waiting for transfers between devices  284 us (46%)
  starting transfers between devices  144 us (23%)
  local copies, waits for them, and re-layouts  95.1 us (16%)
  blocking collectives  43.6 us (7%)
  matrix products  26.7 us (4%)
  other arithmetic  7.1 us (1%)
    ppermute x7, waiting for transfers between devices, body(): lax.ppermute(packed, 'section', [(source, last_section)])  117 us
    all_to_all x8, waiting for transfers between devices, gathered_pieces(): return lax.all_to_all(copies, axis, 0, 0, tiled=True)  89.7 us
    all_to_all x1, waiting for transfers between devices, body(): lax.all_to_all(outgoing, 'dp', split_axis=1, concat_axis=0, tiled=True)  63.2 us
    all_to_all x8, starting transfers between devices, gathered_pieces(): return lax.all_to_all(copies, axis, 0, 0, tiled=True)  54.8 us
    all_to_all x1, starting transfers between devices, gathered_columns(): pieces = lax.all_to_all(copies, axis, 0, 0, tiled=True)  37 us
    all_to_all x1, blocking collectives, body(): lax.all_to_all(jnp.stack(jnp.split(carry_start, lax.axis_size('dp'), axis...  23.7 us
    slice x14, local copies, waits for them, and re-layouts, body(): rows = packed_of[source][:col_width]  22.6 us
    unnamed x147, local copies, waits for them, and re-layouts  20.3 us
  transfers between devices with their start and end apart: 25, of which 11 were waited for; matrix products, arithmetic and copies ran while one was open for 9% of the time, Pallas kernels for 0%

profile of v1, /device:TPU:1, one launch (start us, length us, event | category | flops | bytes accessed | tf_op | source)
XLA Modules:
  0.0 602.1 jit_solution(5663581825155474104)
XLA Ops:
  1.6 2.1 fusion.1
  3.7 4.4 copy.315
  8.1 15.1 %all-to-all-start = ((bf16[2,192,3584]{2,0,1:T(2,128)(2,1)}), bf16[2,192,3584]{2,0,1:T(2,128)(2,1)}, u32[]{:S(2)}, u32[]{:S(2)}) async-start(bf16[2,192,3584]{2,0,1:T(2,128)(2,1)} %copy.315), calls=%async_computation | async-start | bytes 5505024 | tf_op jit(solution)/shard_map/all_to_all | solution.py:50
  25.1 63.2 %all-to-all-done = bf16[2,192,3584]{2,0,1:T(2,128)(2,1)} async-done(((bf16[2,192,3584]{2,0,1:T(2,128)(2,1)}), bf16[2,192,3584]{2,0,1:T(2,128)(2,1)}, u32[]{:S(2)}, u32[]{:S(2)}) %all-to-all-start) | async-done | bytes 2752544 | tf_op jit(solution)/shard_map/all_to_all | solution.py:50
  88.3 5.2 copy.316
  93.5 6.8 %reshape.238 = bf16[128,3,3584]{2,0,1:T(8,128)(2,1)} reshape(bf16[64,2,3,3584]{3,1,0,2:T(2,128)(2,1)} %copy.316) | data formatting | bytes 5505024 | tf_op jit(solution)/shard_map/reshape.5
  100.2 2.7 fusion.37
  103.2 2.4 fusion.2
  105.7 6.8 %convert_element_type.163 = bf16[64,2,3,8,448]{4,3,1,0,2:T(8,128)(2,1)} reshape(bf16[128,1,3,3584]{3,0,2,1:T(8,128)(2,1)} %fusion.2) | data formatting | bytes 5505024 | tf_op jit(solution)/shard_map/convert_element_type | solution.py:91
  112.5 3.6 copy.319
  116.9 4.9 copy.320
  121.8 14.9 %all-to-all-start.1 = ((bf16[512,2,3,449]{3,1,2,0:T(2,128)(2,1)}), bf16[512,2,3,449]{3,1,2,0:T(2,128)(2,1)}, u32[]{:S(2)}, u32[]{:S(2)}) async-start(bf16[512,2,3,449]{3,1,2,0:T(2,128)(2,1)} %copy.320), calls=%async_computation.1 | async-start | bytes 6291456 | tf_op jit(solution)/shard_map/all_to_all | solution.py:99
  136.7 1.9 reshape_squeeze.3
  139.3 4.9 collective-permute-start
  144.9 1.6 collective-permute-start.2
  146.5 1.5 collective-permute-start.3
  148.0 1.6 collective-permute-start.4
  149.6 117.1 %collective-permute-done = bf16[57,64,56]{1,2,0:T(8,128)(2,1)S(1)} collective-permute-done((bf16[57,64,56]{1,2,0:T(8,128)(2,1)S(1)}, bf16[57,64,56]{1,2,0:T(8,128)(2,1)S(1)}, u32[]{:S(2)}, u32[]{:S(2)}) %collective-permute-start) | collective-permute-done | bytes 408608 | tf_op jit(solution)/shard_map/ppermute | solution.py:108
  266.7 1.6 collective-permute-start.5
  269.2 1.9 collective-permute-start.6
  271.1 3.4 fusion.124
  275.5 23.7 %all_to_all.75 = f32[64,1,1,56]{3,2,1,0:T(1,128)S(1)} all-to-all(f32[64,1,1,56]{3,2,1,0:T(1,128)S(1)} %constant_dynamic-update-slice_fusion), channel_id=1, replica_groups=mesh['section'=8,'dp'=64] {'dp'}, dimensions={0} | all-to-all | bytes 28672 | tf_op jit(solution)/shard_map/all_to_all | solution.py:128
  300.6 19.9 %all_to_all.76 = bf16[64,2,1792]{2,1,0:T(2,128)(2,1)S(1)} all-to-all(bf16[64,2,1792]{2,1,0:T(2,128)(2,1)S(1)} %reshape.273), channel_id=1, replica_groups=mesh['section'=8,'dp'=64] {'dp'}, dimensions={0} | all-to-all | bytes 917504 | tf_op jit(solution)/shard_map/all_to_all | solution.py:18
  321.1 2.2 bitcast_convert_fusion.6
  323.4 1.3 reshape.275
  324.7 6.3 %all-to-all-start.5 = ((bf16[64,2,1792]{2,1,0:T(2,128)(2,1)}), bf16[64,2,1792]{2,1,0:T(2,128)(2,1)S(1)}, u32[]{:S(2)}, u32[]{:S(2)}) async-start(bf16[64,2,1792]{2,1,0:T(2,128)(2,1)} %reshape.275), calls=%async_computation.5 | async-start | bytes 917504 | tf_op jit(solution)/shard_map/all_to_all | solution.py:18
  332.3 2.2 copy.329
  334.5 12.5 %all-to-all-done.5 = bf16[64,2,1792]{2,1,0:T(2,128)(2,1)S(1)} async-done(((bf16[64,2,1792]{2,1,0:T(2,128)(2,1)}), bf16[64,2,1792]{2,1,0:T(2,128)(2,1)S(1)}, u32[]{:S(2)}, u32[]{:S(2)}) %all-to-all-start.5) | async-done | bytes 458784 | tf_op jit(solution)/shard_map/all_to_all | solution.py:18
  347.6 1.8 bitcast_convert_fusion.5
  349.4 1.3 reshape.277
  350.8 6.6 %all-to-all-start.6 = ((bf16[64,2,1792]{2,1,0:T(2,128)(2,1)}), bf16[64,2,1792]{2,1,0:T(2,128)(2,1)S(1)}, u32[]{:S(2)}, u32[]{:S(2)}) async-start(bf16[64,2,1792]{2,1,0:T(2,128)(2,1)} %reshape.277), calls=%async_computation.6 | async-start | bytes 917504 | tf_op jit(solution)/shard_map/all_to_all | solution.py:18
  358.6 2.2 copy.330
  360.8 12.4 %all-to-all-done.6 = bf16[64,2,1792]{2,1,0:T(2,128)(2,1)S(1)} async-done(((bf16[64,2,1792]{2,1,0:T(2,128)(2,1)}), bf16[64,2,1792]{2,1,0:T(2,128)(2,1)S(1)}, u32[]{:S(2)}, u32[]{:S(2)}) %all-to-all-start.6) | async-done | bytes 458784 | tf_op jit(solution)/shard_map/all_to_all | solution.py:18
  373.7 1.8 bitcast_convert_fusion.4
  376.9 6.3 %all-to-all-start.7 = ((bf16[64,2,1792]{2,1,0:T(2,128)(2,1)}), bf16[64,2,1792]{2,1,0:T(2,128)(2,1)S(1)}, u32[]{:S(2)}, u32[]{:S(2)}) async-start(bf16[64,2,1792]{2,1,0:T(2,128)(2,1)} %reshape.279), calls=%async_computation.7 | async-start | bytes 917504 | tf_op jit(solution)/shard_map/all_to_all | solution.py:18
  384.4 2.2 copy.331
  386.6 12.5 %all-to-all-done.7 = bf16[64,2,1792]{2,1,0:T(2,128)(2,1)S(1)} async-done(((bf16[64,2,1792]{2,1,0:T(2,128)(2,1)}), bf16[64,2,1792]{2,1,0:T(2,128)(2,1)S(1)}, u32[]{:S(2)}, u32[]{:S(2)}) %all-to-all-start.7) | async-done | bytes 458784 | tf_op jit(solution)/shard_map/all_to_all | solution.py:18
  399.6 1.7 bitcast_convert_fusion.3
  402.9 6.3 %all-to-all-start.8 = ((bf16[64,2,1792]{2,1,0:T(2,128)(2,1)}), bf16[64,2,1792]{2,1,0:T(2,128)(2,1)S(1)}, u32[]{:S(2)}, u32[]{:S(2)}) async-start(bf16[64,2,1792]{2,1,0:T(2,128)(2,1)} %reshape.281), calls=%async_computation.8 | async-start | bytes 917504 | tf_op jit(solution)/shard_map/all_to_all | solution.py:18
  410.4 2.2 copy.332
  412.6 12.5 %all-to-all-done.8 = bf16[64,2,1792]{2,1,0:T(2,128)(2,1)S(1)} async-done(((bf16[64,2,1792]{2,1,0:T(2,128)(2,1)}), bf16[64,2,1792]{2,1,0:T(2,128)(2,1)S(1)}, u32[]{:S(2)}, u32[]{:S(2)}) %all-to-all-start.8) | async-done | bytes 458784 | tf_op jit(solution)/shard_map/all_to_all | solution.py:18
  425.6 1.8 bitcast_convert_fusion.2
  428.8 6.6 %all-to-all-start.9 = ((bf16[64,2,1792]{2,1,0:T(2,128)(2,1)}), bf16[64,2,1792]{2,1,0:T(2,128)(2,1)S(1)}, u32[]{:S(2)}, u32[]{:S(2)}) async-start(bf16[64,2,1792]{2,1,0:T(2,128)(2,1)} %reshape.283), calls=%async_computation.9 | async-start | bytes 917504 | tf_op jit(solution)/shard_map/all_to_all | solution.py:18
  436.7 2.2 copy.333
  438.9 12.4 %all-to-all-done.9 = bf16[64,2,1792]{2,1,0:T(2,128)(2,1)S(1)} async-done(((bf16[64,2,1792]{2,1,0:T(2,128)(2,1)}), bf16[64,2,1792]{2,1,0:T(2,128)(2,1)S(1)}, u32[]{:S(2)}, u32[]{:S(2)}) %all-to-all-start.9) | async-done | bytes 458784 | tf_op jit(solution)/shard_map/all_to_all | solution.py:18
  451.8 1.7 bitcast_convert_fusion.1
  455.0 6.3 %all-to-all-start.10 = ((bf16[64,2,1792]{2,1,0:T(2,128)(2,1)}), bf16[64,2,1792]{2,1,0:T(2,128)(2,1)S(1)}, u32[]{:S(2)}, u32[]{:S(2)}) async-start(bf16[64,2,1792]{2,1,0:T(2,128)(2,1)} %reshape.285), calls=%async_computation.10 | async-start | bytes 917504 | tf_op jit(solution)/shard_map/all_to_all | solution.py:18
  462.5 2.2 copy.334
  464.7 12.5 %all-to-all-done.10 = bf16[64,2,1792]{2,1,0:T(2,128)(2,1)S(1)} async-done(((bf16[64,2,1792]{2,1,0:T(2,128)(2,1)}), bf16[64,2,1792]{2,1,0:T(2,128)(2,1)S(1)}, u32[]{:S(2)}, u32[]{:S(2)}) %all-to-all-start.10) | async-done | bytes 458784 | tf_op jit(solution)/shard_map/all_to_all | solution.py:18
  478.9 1.3 reshape.287
  480.3 6.3 %all-to-all-start.11 = ((bf16[64,2,1792]{2,1,0:T(2,128)(2,1)}), bf16[64,2,1792]{2,1,0:T(2,128)(2,1)S(1)}, u32[]{:S(2)}, u32[]{:S(2)}) async-start(bf16[64,2,1792]{2,1,0:T(2,128)(2,1)} %reshape.287), calls=%async_computation.11 | async-start | bytes 917504 | tf_op jit(solution)/shard_map/all_to_all | solution.py:18
  486.6 8.7 %copy.322 = bf16[512,2,3,449]{0,3,2,1:T(8,128)(2,1)} copy(bf16[512,2,3,449]{3,1,2,0:T(2,128)(2,1)} %all-to-all-done.1) | data formatting | bytes 5517312 | tf_op jit(solution)/shard_map/optimization_barrier | solution.py:112
  496.0 2.7 fusion.10
  498.9 3.6 all-to-all-done.11
  503.6 37.0 %all-to-all-start.2 = ((bf16[8,128,448]{1,2,0:T(8,128)(2,1)}), bf16[8,128,448]{1,2,0:T(8,128)(2,1)S(1)}, u32[]{:S(2)}, u32[]{:S(2)}) async-start(bf16[8,128,448]{1,2,0:T(8,128)(2,1)} %broadcast_in_dim.137), calls=%async_computation.2 | async-start | bytes 1835008 | tf_op jit(solution)/shard_map/all_to_all | solution.py:24
  540.7 2.2 copy.335
  554.3 13.6 %collective-permute-done.13 = f32[2,64,56]{1,2,0:T(8,128)S(1)} collective-permute-done((f32[2,64,56]{1,2,0:T(8,128)S(1)}, f32[2,64,56]{1,2,0:T(8,128)S(1)}, u32[]{:S(2)}, u32[]{:S(2)}) %collective-permute-start.13) | collective-permute-done | bytes 28704 | tf_op jit(solution)/shard_map/ppermute | solution.py:148
  568.8 1.3 reshape.289
  570.2 10.1 %all-to-all-start.12 = ((bf16[64,2,1792]{2,1,0:T(2,128)(2,1)}), bf16[64,2,1792]{2,1,0:T(2,128)(2,1)S(1)}, u32[]{:S(2)}, u32[]{:S(2)}) async-start(bf16[64,2,1792]{2,1,0:T(2,128)(2,1)} %reshape.289), calls=%async_computation.12 | async-start | bytes 917504 | tf_op jit(solution)/shard_map/all_to_all | solution.py:18
  581.4 2.1 reshape_reshape.8
  583.5 1.5 fusion.107
  585.0 11.2 %all-to-all-done.12 = bf16[64,2,1792]{2,1,0:T(2,128)(2,1)S(1)} async-done(((bf16[64,2,1792]{2,1,0:T(2,128)(2,1)}), bf16[64,2,1792]{2,1,0:T(2,128)(2,1)S(1)}, u32[]{:S(2)}, u32[]{:S(2)}) %all-to-all-start.12) | async-done | bytes 458784 | tf_op jit(solution)/shard_map/all_to_all | solution.py:18
  597.8 1.4 copy.337
  599.2 2.5 convert_element_type.195
  (205 shorter events, 43.4 us)
Async XLA Ops:
  0.6 99.6 %copy-start = (bf16[128,3584]{1,0:T(8,128)(2,1)S(1)}, bf16[128,3584]{1,0:T(8,128)(2,1)}, u32[]{:S(2)}) copy-start(bf16[128,3584]{1,0:T(8,128)(2,1)} %param.8) | copy-start | bytes 2752516
  8.1 15.2 %copy-start.11 = (f32[128,384]{1,0:T(8,128)S(1)}, f32[128,384]{1,0:T(8,128)}, u32[]{:S(2)}) copy-start(f32[128,384]{1,0:T(8,128)} %param.12) | copy-start | bytes 589828
  8.1 15.3 %copy-start.26 = (s32[64]{0:T(128)S(1)}, s32[64]{0:T(128)}, u32[]{:S(2)}) copy-start(s32[64]{0:T(128)} %param.11) | copy-start | bytes 772
  8.1 80.2 %all-to-all-start = ((bf16[2,192,3584]{2,0,1:T(2,128)(2,1)}), bf16[2,192,3584]{2,0,1:T(2,128)(2,1)}, u32[]{:S(2)}, u32[]{:S(2)}) async-start(bf16[2,192,3584]{2,0,1:T(2,128)(2,1)} %copy.315), calls=%async_computation | async-start | bytes 5505024 | tf_op jit(solution)/shard_map/all_to_all | solution.py:50
  121.8 14.9 %copy-start.5 = (bf16[1,56,3584]{2,1,0:T(8,128)(2,1)S(1)}, bf16[1,56,3584]{2,1,0:T(8,128)(2,1)}, u32[]{:S(2)}) copy-start(bf16[1,56,3584]{2,1,0:T(8,128)(2,1)} %param.13) | copy-start | bytes 1204228
  121.8 152.9 %all-to-all-start.1 = ((bf16[512,2,3,449]{3,1,2,0:T(2,128)(2,1)}), bf16[512,2,3,449]{3,1,2,0:T(2,128)(2,1)}, u32[]{:S(2)}, u32[]{:S(2)}) async-start(bf16[512,2,3,449]{3,1,2,0:T(2,128)(2,1)} %copy.320), calls=%async_computation.1 | async-start | bytes 6291456 | tf_op jit(solution)/shard_map/all_to_all | solution.py:99
  136.7 2.5 copy-start.22
  139.3 127.4 %collective-permute-start = (bf16[57,64,56]{1,2,0:T(8,128)(2,1)S(1)}, bf16[57,64,56]{1,2,0:T(8,128)(2,1)S(1)}, u32[]{:S(2)}, u32[]{:S(2)}) collective-permute-start(bf16[57,64,56]{1,2,0:T(8,128)(2,1)S(1)} %pad_maximum_fusion.1), channel_id=1, source_target_pairs={{0,448},{1,449},{2,450},{3,451},{4,452},{5,453},{6,454},{7,455},{8... | collective-permute-start | bytes 1225736 | tf_op jit(solution)/shard_map/ppermute | solution.py:108
  144.2 124.1 %collective-permute-start.1 = (bf16[57,64,56]{1,2,0:T(8,128)(2,1)S(1)}, bf16[57,64,56]{1,2,0:T(8,128)(2,1)S(1)}, u32[]{:S(2)}, u32[]{:S(2)}) collective-permute-start(bf16[57,64,56]{1,2,0:T(8,128)(2,1)S(1)} %pad_maximum_fusion.1), channel_id=1, source_target_pairs={{64,448},{65,449},{66,450},{67,451},{68,452},{69,453},{70,454},{71... | collective-permute-start | bytes 1225736 | tf_op jit(solution)/shard_map/ppermute | solution.py:108
  144.9 129.7 %collective-permute-start.2 = (bf16[57,64,56]{1,2,0:T(8,128)(2,1)S(1)}, bf16[57,64,56]{1,2,0:T(8,128)(2,1)}, u32[]{:S(2)}, u32[]{:S(2)}) collective-permute-start(bf16[57,64,56]{1,2,0:T(8,128)(2,1)S(1)} %pad_maximum_fusion.1), channel_id=1, source_target_pairs={{128,448},{129,449},{130,450},{131,451},{132,452},{133,453},{134,4... | collective-permute-start | bytes 1225736 | tf_op jit(solution)/shard_map/ppermute | solution.py:108
  146.5 128.1 %collective-permute-start.3 = (bf16[57,64,56]{1,2,0:T(8,128)(2,1)S(1)}, bf16[57,64,56]{1,2,0:T(8,128)(2,1)}, u32[]{:S(2)}, u32[]{:S(2)}) collective-permute-start(bf16[57,64,56]{1,2,0:T(8,128)(2,1)S(1)} %pad_maximum_fusion.1), channel_id=1, source_target_pairs={{192,448},{193,449},{194,450},{195,451},{196,452},{197,453},{198,4... | collective-permute-start | bytes 1225736 | tf_op jit(solution)/shard_map/ppermute | solution.py:108
  148.0 126.6 %collective-permute-start.4 = (bf16[57,64,56]{1,2,0:T(8,128)(2,1)S(1)}, bf16[57,64,56]{1,2,0:T(8,128)(2,1)}, u32[]{:S(2)}, u32[]{:S(2)}) collective-permute-start(bf16[57,64,56]{1,2,0:T(8,128)(2,1)S(1)} %pad_maximum_fusion.1), channel_id=1, source_target_pairs={{256,448},{257,449},{258,450},{259,451},{260,452},{261,453},{262,4... | collective-permute-start | bytes 1225736 | tf_op jit(solution)/shard_map/ppermute | solution.py:108
  266.7 211.0 %copy-start.2 = (bf16[57,64,56]{1,2,0:T(8,128)(2,1)}, bf16[57,64,56]{1,2,0:T(8,128)(2,1)S(1)}, u32[]{:S(2)}) copy-start(bf16[57,64,56]{1,2,0:T(8,128)(2,1)S(1)} %collective-permute-done) | copy-start | bytes 1225732
  266.7 7.9 %collective-permute-start.5 = (bf16[57,64,56]{1,2,0:T(8,128)(2,1)S(1)}, bf16[57,64,56]{1,2,0:T(8,128)(2,1)}, u32[]{:S(2)}, u32[]{:S(2)}) collective-permute-start(bf16[57,64,56]{1,2,0:T(8,128)(2,1)S(1)} %pad_maximum_fusion.1), channel_id=1, source_target_pairs={{320,448},{321,449},{322,450},{323,451},{324,452},{325,453},{326,4... | collective-permute-start | bytes 1225736 | tf_op jit(solution)/shard_map/ppermute | solution.py:108
  268.3 0.9 copy-start.4
  269.2 5.5 collective-permute-start.6
  299.3 0.6 copy-start.12
  323.3 24.3 %copy-start.20 = (f32[64,56]{0,1:T(8,128)}, f32[64,56]{0,1:T(8,128)S(1)}, u32[]{:S(2)}) copy-start(f32[64,56]{0,1:T(8,128)S(1)} %get-tuple-element.40) | copy-start | bytes 43012
  324.7 22.3 %all-to-all-start.5 = ((bf16[64,2,1792]{2,1,0:T(2,128)(2,1)}), bf16[64,2,1792]{2,1,0:T(2,128)(2,1)S(1)}, u32[]{:S(2)}, u32[]{:S(2)}) async-start(bf16[64,2,1792]{2,1,0:T(2,128)(2,1)} %reshape.275), calls=%async_computation.5 | async-start | bytes 917504 | tf_op jit(solution)/shard_map/all_to_all | solution.py:18
  350.8 22.4 %all-to-all-start.6 = ((bf16[64,2,1792]{2,1,0:T(2,128)(2,1)}), bf16[64,2,1792]{2,1,0:T(2,128)(2,1)S(1)}, u32[]{:S(2)}, u32[]{:S(2)}) async-start(bf16[64,2,1792]{2,1,0:T(2,128)(2,1)} %reshape.277), calls=%async_computation.6 | async-start | bytes 917504 | tf_op jit(solution)/shard_map/all_to_all | solution.py:18
  376.9 22.2 %all-to-all-start.7 = ((bf16[64,2,1792]{2,1,0:T(2,128)(2,1)}), bf16[64,2,1792]{2,1,0:T(2,128)(2,1)S(1)}, u32[]{:S(2)}, u32[]{:S(2)}) async-start(bf16[64,2,1792]{2,1,0:T(2,128)(2,1)} %reshape.279), calls=%async_computation.7 | async-start | bytes 917504 | tf_op jit(solution)/shard_map/all_to_all | solution.py:18
  402.9 22.2 %all-to-all-start.8 = ((bf16[64,2,1792]{2,1,0:T(2,128)(2,1)}), bf16[64,2,1792]{2,1,0:T(2,128)(2,1)S(1)}, u32[]{:S(2)}, u32[]{:S(2)}) async-start(bf16[64,2,1792]{2,1,0:T(2,128)(2,1)} %reshape.281), calls=%async_computation.8 | async-start | bytes 917504 | tf_op jit(solution)/shard_map/all_to_all | solution.py:18
  427.4 24.4 %copy-start.6 = (f32[64,56]{0,1:T(8,128)}, f32[64,56]{0,1:T(8,128)S(1)}, u32[]{:S(2)}) copy-start(f32[64,56]{0,1:T(8,128)S(1)} %get-tuple-element.44) | copy-start | bytes 43012
  428.8 22.4 %all-to-all-start.9 = ((bf16[64,2,1792]{2,1,0:T(2,128)(2,1)}), bf16[64,2,1792]{2,1,0:T(2,128)(2,1)S(1)}, u32[]{:S(2)}, u32[]{:S(2)}) async-start(bf16[64,2,1792]{2,1,0:T(2,128)(2,1)} %reshape.283), calls=%async_computation.9 | async-start | bytes 917504 | tf_op jit(solution)/shard_map/all_to_all | solution.py:18
  453.5 24.2 %copy-start.8 = (f32[64,56]{0,1:T(8,128)}, f32[64,56]{0,1:T(8,128)S(1)}, u32[]{:S(2)}) copy-start(f32[64,56]{0,1:T(8,128)S(1)} %get-tuple-element.45) | copy-start | bytes 43012
  455.0 22.2 %all-to-all-start.10 = ((bf16[64,2,1792]{2,1,0:T(2,128)(2,1)}), bf16[64,2,1792]{2,1,0:T(2,128)(2,1)S(1)}, u32[]{:S(2)}, u32[]{:S(2)}) async-start(bf16[64,2,1792]{2,1,0:T(2,128)(2,1)} %reshape.285), calls=%async_computation.10 | async-start | bytes 917504 | tf_op jit(solution)/shard_map/all_to_all | solution.py:18
  480.3 22.2 %all-to-all-start.11 = ((bf16[64,2,1792]{2,1,0:T(2,128)(2,1)}), bf16[64,2,1792]{2,1,0:T(2,128)(2,1)S(1)}, u32[]{:S(2)}, u32[]{:S(2)}) async-start(bf16[64,2,1792]{2,1,0:T(2,128)(2,1)} %reshape.287), calls=%async_computation.11 | async-start | bytes 917504 | tf_op jit(solution)/shard_map/all_to_all | solution.py:18
  496.0 44.6 %copy-start.3 = (bf16[57,64,56]{1,2,0:T(8,128)(2,1)S(1)}, bf16[57,64,56]{1,2,0:T(8,128)(2,1)}, u32[]{:S(2)}) copy-start(bf16[57,64,56]{1,2,0:T(8,128)(2,1)} %copy-done.2) | copy-start | bytes 1225732
  503.5 39.4 %copy-start.24 = (f32[1,64,56]{1,2,0:T(8,128)S(1)}, f32[1,64,56]{1,2,0:T(8,128)}, u32[]{:S(2)}) copy-start(f32[1,64,56]{1,2,0:T(8,128)} %get-tuple-element.22) | copy-start | bytes 43012
  503.5 41.3 %copy-start.14 = (f32[1,64,56]{1,2,0:T(8,128)S(1)}, f32[1,64,56]{1,2,0:T(8,128)}, u32[]{:S(2)}) copy-start(f32[1,64,56]{1,2,0:T(8,128)} %get-tuple-element.24) | copy-start | bytes 43012
  503.5 43.2 %copy-start.15 = (f32[1,64,56]{1,2,0:T(8,128)S(1)}, f32[1,64,56]{1,2,0:T(8,128)}, u32[]{:S(2)}) copy-start(f32[1,64,56]{1,2,0:T(8,128)} %get-tuple-element.26) | copy-start | bytes 43012
  503.5 44.5 %copy-start.7 = (f32[64,56]{0,1:T(8,128)S(1)}, f32[64,56]{0,1:T(8,128)}, u32[]{:S(2)}) copy-start(f32[64,56]{0,1:T(8,128)} %copy-done.6) | copy-start | bytes 43012
  503.6 44.5 %copy-start.16 = (f32[1,64,56]{1,2,0:T(8,128)S(1)}, f32[1,64,56]{1,2,0:T(8,128)}, u32[]{:S(2)}) copy-start(f32[1,64,56]{1,2,0:T(8,128)} %get-tuple-element.28) | copy-start | bytes 43012
  503.6 45.7 %copy-start.9 = (f32[64,56]{0,1:T(8,128)S(1)}, f32[64,56]{0,1:T(8,128)}, u32[]{:S(2)}) copy-start(f32[64,56]{0,1:T(8,128)} %copy-done.8) | copy-start | bytes 43012
  503.6 45.7 %copy-start.17 = (f32[1,64,56]{1,2,0:T(8,128)S(1)}, f32[1,64,56]{1,2,0:T(8,128)}, u32[]{:S(2)}) copy-start(f32[1,64,56]{1,2,0:T(8,128)} %get-tuple-element.30) | copy-start | bytes 43012
  503.6 47.0 %copy-start.10 = (f32[64,56]{0,1:T(8,128)S(1)}, f32[64,56]{0,1:T(8,128)}, u32[]{:S(2)}) copy-start(f32[64,56]{0,1:T(8,128)} %get-tuple-element.46) | copy-start | bytes 43012
  503.6 47.0 %copy-start.18 = (f32[1,64,56]{1,2,0:T(8,128)S(1)}, f32[1,64,56]{1,2,0:T(8,128)}, u32[]{:S(2)}) copy-start(f32[1,64,56]{1,2,0:T(8,128)} %get-tuple-element.32) | copy-start | bytes 43012
  503.6 66.6 %all-to-all-start.2 = ((bf16[8,128,448]{1,2,0:T(8,128)(2,1)}), bf16[8,128,448]{1,2,0:T(8,128)(2,1)S(1)}, u32[]{:S(2)}, u32[]{:S(2)}) async-start(bf16[8,128,448]{1,2,0:T(8,128)(2,1)} %broadcast_in_dim.137), calls=%async_computation.2 | async-start | bytes 1835008 | tf_op jit(solution)/shard_map/all_to_all | solution.py:24
  540.7 11.5 %copy-start.19 = (f32[1,64,56]{1,2,0:T(8,128)S(1)}, f32[1,64,56]{1,2,0:T(8,128)}, u32[]{:S(2)}) copy-start(f32[1,64,56]{1,2,0:T(8,128)} %get-tuple-element.34) | copy-start | bytes 43012
  540.7 27.2 %copy-start.13 = (bf16[1,64,56]{1,2,0:T(8,128)(2,1)S(1)}, bf16[1,64,56]{1,2,0:T(8,128)(2,1)}, u32[]{:S(2)}) copy-start(bf16[1,64,56]{1,2,0:T(8,128)(2,1)} %copy-done.12) | copy-start | bytes 21508
  543.5 8.7 %collective-permute-start.7 = (f32[2,64,56]{1,2,0:T(8,128)}, f32[2,64,56]{1,2,0:T(8,128)}, u32[]{:S(2)}, u32[]{:S(2)}) collective-permute-start(f32[2,64,56]{1,2,0:T(8,128)} %pad_maximum_fusion.2), channel_id=1, source_target_pairs={{448,384},{449,385},{450,386},{451,387},{452,388},{453,389},{454,3... | collective-permute-start | bytes 86024 | tf_op jit(solution)/shard_map/ppermute | solution.py:148
  545.4 7.5 %collective-permute-start.8 = (f32[2,64,56]{1,2,0:T(8,128)}, f32[2,64,56]{1,2,0:T(8,128)}, u32[]{:S(2)}, u32[]{:S(2)}) collective-permute-start(f32[2,64,56]{1,2,0:T(8,128)} %pad_maximum_fusion.3), channel_id=1, source_target_pairs={{448,320},{449,321},{450,322},{451,323},{452,324},{453,325},{454,3... | collective-permute-start | bytes 86024 | tf_op jit(solution)/shard_map/ppermute | solution.py:148
  546.7 7.5 %collective-permute-start.9 = (f32[2,64,56]{1,2,0:T(8,128)S(1)}, f32[2,64,56]{1,2,0:T(8,128)}, u32[]{:S(2)}, u32[]{:S(2)}) collective-permute-start(f32[2,64,56]{1,2,0:T(8,128)S(1)} %pad_maximum_fusion.4), channel_id=1, source_target_pairs={{448,256},{449,257},{450,258},{451,259},{452,260},{453,261},{454,2... | collective-permute-start | bytes 86024 | tf_op jit(solution)/shard_map/ppermute | solution.py:148
  548.0 6.3 %collective-permute-start.10 = (f32[2,64,56]{1,2,0:T(8,128)S(1)}, f32[2,64,56]{1,2,0:T(8,128)}, u32[]{:S(2)}, u32[]{:S(2)}) collective-permute-start(f32[2,64,56]{1,2,0:T(8,128)S(1)} %pad_maximum_fusion.5), channel_id=1, source_target_pairs={{448,192},{449,193},{450,194},{451,195},{452,196},{453,197},{454,1... | collective-permute-start | bytes 86024 | tf_op jit(solution)/shard_map/ppermute | solution.py:148
  549.3 5.0 collective-permute-start.11
  551.2 1.0 copy-start.23
  552.3 2.0 collective-permute-start.12
  552.9 14.9 %collective-permute-start.13 = (f32[2,64,56]{1,2,0:T(8,128)S(1)}, f32[2,64,56]{1,2,0:T(8,128)S(1)}, u32[]{:S(2)}, u32[]{:S(2)}) collective-permute-start(f32[2,64,56]{1,2,0:T(8,128)S(1)} %pad_maximum_fusion.8), channel_id=1, source_target_pairs={{448,0},{449,1},{450,2},{451,3},{452,4},{453,5},{454,6},{455,7},{4... | collective-permute-start | bytes 86024 | tf_op jit(solution)/shard_map/ppermute | solution.py:148
  570.2 13.3 %copy-start.21 = (f32[64,56]{0,1:T(8,128)S(1)}, f32[64,56]{0,1:T(8,128)}, u32[]{:S(2)}) copy-start(f32[64,56]{0,1:T(8,128)} %copy-done.20) | copy-start | bytes 43012
  570.2 26.1 %all-to-all-start.12 = ((bf16[64,2,1792]{2,1,0:T(2,128)(2,1)}), bf16[64,2,1792]{2,1,0:T(2,128)(2,1)S(1)}, u32[]{:S(2)}, u32[]{:S(2)}) async-start(bf16[64,2,1792]{2,1,0:T(2,128)(2,1)} %reshape.289), calls=%async_computation.12 | async-start | bytes 917504 | tf_op jit(solution)/shard_map/all_to_all | solution.py:18
  580.3 16.5 %copy-start.25 = (bf16[1,64,56]{1,2,0:T(8,128)(2,1)S(1)}, bf16[1,64,56]{1,2,0:T(8,128)(2,1)}, u32[]{:S(2)}) copy-start(bf16[1,64,56]{1,2,0:T(8,128)(2,1)} %param.14) | copy-start | bytes 21508
  583.5 18.2 %copy-start.1 = (bf16[128,3584]{1,0:T(8,128)(2,1)S(1)}, bf16[128,3584]{1,0:T(8,128)(2,1)}, u32[]{:S(2)}) copy-start(bf16[128,3584]{1,0:T(8,128)(2,1)} %param.8) | copy-start | bytes 2752516
